TPU v7x, 128 devices: a whole 4x4x4 slice. The times are simulated.
128 devices in a mesh: term: 4 (over x_hi, core), sec: 32 (over x_lo, z, y).
Axes of the slice: x: 4 (x_hi: 2, x_lo: 2; x = x_hi * 2 + x_lo), y: 4, z: 4, core: 2. Of those that a mesh axis runs over, the one named last changes fastest.
Arguments:
- psi_tiles: bfloat16 [768, 512, 512], P('sec'), may hold values from -6 to 6
- sectors: int32 [768, 2], P('sec'), may hold values from 0 to 15
- sources: int32 [4, 768], P('term', 'sec'), may hold values from 0 to 767, as said below
- left_env: bfloat16 [4, 16, 512, 512], P('term', None, 'sec'), may hold values from -0.25 to 0.25
- right_env: bfloat16 [4, 16, 512, 512], P('term', None, 'sec'), may hold values from -0.25 to 0.25
Outputs:
- applied: bfloat16 [768, 512, 512], P('sec', 'term')
Inputs may be any that keep to these rules, and one draw needn't show every extreme that they name: sources[t, k] lies in the same aligned block of 24 tiles as k, and each row maps each such block one to one onto itself.
All inputs are finite; a program needn't handle non-finite values.
Results may differ from a plain program's by a relative error of at most 0.013.
Values may be sent and summed in bfloat16 or wider, within the bound.
No kernel may reach another device: no remote copies, remote signals or barrier semaphores. Data moves between devices by JAX's collectives and lax.ppermute only.
A program may use at most 192 MiB of HBM per device.

v0:
```python
import jax
import jax.numpy as jnp
from jax import lax
from jax.sharding import PartitionSpec as P


def body(psi_tiles, sectors, sources, left_env, right_env):
    tile_count = psi_tiles.shape[0]
    width = psi_tiles.shape[2]
    local_ids = sources[0] - lax.axis_index("sec") * tile_count
    moved = jnp.take(psi_tiles, local_ids, axis=0)
    left_ids = sectors[:, 0]
    right_ids = sectors[:, 1]
    chosen = jnp.take(lax.all_gather(right_env[0], "sec", axis=1, tiled=True), right_ids, axis=0)
    half = jnp.einsum("kij,kjl->kil", moved, chosen, preferred_element_type=jnp.float32).astype(
        jnp.bfloat16
    )
    chosen = jnp.take(lax.all_gather(left_env[0], "sec", axis=1, tiled=True), left_ids, axis=0)
    term_out = jnp.einsum("kij,kjl->kil", chosen, half, preferred_element_type=jnp.float32)
    share_rows = width // lax.axis_size("term")
    summed = lax.psum(term_out.astype(jnp.bfloat16), "term").astype(jnp.float32)
    kept = lax.dynamic_slice_in_dim(summed, lax.axis_index("term") * share_rows, share_rows, 1)
    return kept.astype(jnp.bfloat16)


def solution(mesh):
    placed = (
        P("sec", None, None),
        P("sec", None),
        P("term", "sec"),
        P("term", None, "sec", None),
        P("term", None, "sec", None),
    )
    return jax.shard_map(
        body, mesh=mesh, in_specs=placed, out_specs=P("sec", "term", None), check_vma=False
    )
```

profile of v0, /device:TPU:1, one launch (start us, length us, event | category | flops | bytes accessed | tf_op | source)
XLA Modules:
  0.0 617.2 jit_solution(6412177317776371115)
XLA Ops:
  6.5 0.0 all-gather.7.cloned.1.call-start
  6.5 0.7 all-gather.7.cloned.1.call-update
  7.3 0.0 all-gather.5.cloned.1.call-start
  7.3 0.7 all-gather.5.cloned.1.call-update
  8.0 0.0 all-reduce.2.cloned.1.call-start
  8.1 0.7 fusion.30
  8.7 0.0 copy-start
  8.7 0.0 copy-start.1
  8.7 10.6 %gather_fusion = bf16[24,512,512]{2,1,0:T(8,128)(2,1)} fusion(bf16[24,512,512]{2,1,0:T(8,128)(2,1)} %param.7, s32[1024]{0:T(1024)S(1)} %pad_clamp_fusion.1), kind=kCustom, calls=%fused_computation.2 | custom fusion | bytes 25165920 | tf_op jit(solution)/shard_map/jit(_take)/gather | solution.py:11
  19.4 0.0 copy-done
  19.4 0.0 copy-done.1
  19.4 138.6 %all-gather.7.cloned.1.call-done = bf16[1,16,512,512]{3,2,1,0:T(8,128)(2,1)} async-done(((bf16[1,16,16,512]{3,2,1,0:T(8,128)(2,1)}), bf16[1,16,512,512]{3,2,1,0:T(8,128)(2,1)}) %all-gather.7.cloned.1.call-update) | async-done | bytes 8388624 | tf_op jit(solution)/shard_map/all_gather | solution.py:14
  158.0 9.5 %gather_fusion.2 = bf16[24,512,512]{2,1,0:T(8,128)(2,1)} fusion(bf16[16,512,512]{2,1,0:T(8,128)(2,1)} %bitcast.14, s32[1024]{0:T(1024)S(1)} %get-tuple-element.12), kind=kCustom, calls=%fused_computation.1.clone | custom fusion | bytes 25165920 | tf_op jit(solution)/shard_map/jit(_take)/gather | solution.py:14
  167.4 158.8 %all-gather.5.cloned.1.call-done = bf16[1,16,512,512]{3,2,1,0:T(8,128)(2,1)} async-done(((bf16[1,16,16,512]{3,2,1,0:T(8,128)(2,1)}), bf16[1,16,512,512]{3,2,1,0:T(8,128)(2,1)}) %all-gather.5.cloned.1.call-update) | async-done | bytes 8388624 | tf_op jit(solution)/shard_map/all_gather | solution.py:18
  326.3 9.5 %gather_fusion.1 = bf16[24,512,512]{2,1,0:T(8,128)(2,1)} fusion(bf16[16,512,512]{2,1,0:T(8,128)(2,1)} %bitcast.15, s32[1024]{0:T(1024)S(1)} %get-tuple-element.13), kind=kCustom, calls=%fused_computation.clone | custom fusion | bytes 25165920 | tf_op jit(solution)/shard_map/jit(_take)/gather | solution.py:18
  335.8 21.7 %fusion.19 = bf16[24,512,512]{2,1,0:T(8,128)(2,1)} fusion(bf16[24,512,512]{2,1,0:T(8,128)(2,1)} %gather_fusion.2, bf16[24,512,512]{2,1,0:T(8,128)(2,1)} %gather_fusion, pred[24]{0:T(512)(128)(4,1)S(1)} %get-tuple-element.10, pred[24]{0:T(512)(128)(4,1)S(1)} %compare_and_fusion.2, bf16[24,512,512]{2,1,0:T(8,128)(2,1)} %gather_fusion.1, ...), kind=kOutput, calls=%fused_computation.12 | convolution fusion | flops 12916359168 | bytes 50331720 | tf_op jit(solution)/shard_map/kij,kjl->kil/dot_general | solution.py:19
  357.5 0.0 all-reduce.2.cloned.1.call-update
  357.5 249.3 %all-reduce.2.cloned.1.call-done = bf16[24,512,512]{2,1,0:T(8,128)(2,1)} async-done(((bf16[24,512,512]{2,1,0:T(8,128)(2,1)}), bf16[24,512,512]{2,1,0:T(8,128)(2,1)}) %all-reduce.2.cloned.1.call-update) | async-done | bytes 12582928 | tf_op jit(solution)/shard_map/psum | solution.py:21
  606.8 3.9 convert_convert_fusion
  (4 shorter events, 0.0 us)
Async XLA Ops:
  6.5 151.4 %all-gather.7.cloned.1.call-start = ((), (), s32[]{:S(2)}) async-start(), calls=%async_computation.2 | async-start | bytes 8650752 | tf_op jit(solution)/shard_map/all_gather | solution.py:14
  7.3 319.0 %all-gather.5.cloned.1.call-start = ((), (), s32[]{:S(2)}) async-start(), calls=%async_computation.1 | async-start | bytes 8650752 | tf_op jit(solution)/shard_map/all_gather | solution.py:18
  8.0 598.8 %all-reduce.2.cloned.1.call-start = ((), (), s32[]{:S(2)}) async-start(), calls=%async_computation | async-start | bytes 25165824 | tf_op jit(solution)/shard_map/psum | solution.py:21
  8.7 10.6 %copy-start = (s32[24,2]{0,1:T(2,128)S(1)}, s32[24,2]{0,1:T(2,128)}, u32[]{:S(2)}) copy-start(s32[24,2]{0,1:T(2,128)} %param.8) | copy-start | bytes 580
  8.7 10.6 %copy-start.1 = (s32[1,24]{1,0:T(1,128)S(1)}, s32[1,24]{1,0:T(1,128)}, u32[]{:S(2)}) copy-start(s32[1,24]{1,0:T(1,128)} %param.9) | copy-start | bytes 292
Sparse Core Ops, SparseCore 0:
  9.0 148.9 all-gather.6
  159.6 166.6 all-gather.4
  357.6 249.1 all-reduce.1
where the time goes:
time: 617 us
  waiting for transfers between devices  548 us (89%)
  local copies, waits for them, and re-layouts  29.6 us (5%)
  matrix products  21.7 us (4%)
  between operations  13.2 us (2%)
    psum x1, waiting for transfers between devices, body(): summed = lax.psum(term_out.astype(jnp.bfloat16), 'term').astype(jnp.float32)  249 us
    all_gather x1, waiting for transfers between devices, body(): lax.all_gather(left_env[0], 'sec', axis=1, tiled=True)  159 us
    all_gather x1, waiting for transfers between devices, body(): lax.all_gather(right_env[0], 'sec', axis=1, tiled=True)  139 us
    dot_general x1, matrix products, body(): jnp.einsum('kij,kjl->kil', chosen, half, preferred_element_type=jnp.float32)  21.7 us
  transfers between devices with their start and end apart: 3, of which 3 were waited for; matrix products, arithmetic and copies ran while one was open for 3% of the time, Pallas kernels for 0%

commit v1 on v0

--- a/solution.py
+++ b/solution.py
@@ -18,7 +18,9 @@
     chosen = jnp.take(lax.all_gather(left_env[0], "sec", axis=1, tiled=True), left_ids, axis=0)
     term_out = jnp.einsum("kij,kjl->kil", chosen, half, preferred_element_type=jnp.float32)
     share_rows = width // lax.axis_size("term")
-    summed = lax.psum(term_out.astype(jnp.bfloat16), "term").astype(jnp.float32)
+    summed = jnp.sum(lax.all_gather(term_out.astype(jnp.bfloat16), "term"), axis=0).astype(
+        jnp.float32
+    )
     kept = lax.dynamic_slice_in_dim(summed, lax.axis_index("term") * share_rows, share_rows, 1)
     return kept.astype(jnp.bfloat16)
 

time: 617 us -> 714 us (1.16)
  waiting for transfers between devices: 548 us -> 621 us
  other arithmetic: 4.55 us -> 27.8 us
    all_gather x0 -> x1, waiting for transfers between devices: none -> 323 us  [body(): lax.all_gather(term_out.astype(jnp.bfloat16), 'term')]
    psum x1 -> x0, waiting for transfers between devices: 249 us -> none  [body(): summed = lax.psum(term_out.astype(jnp.bfloat16), 'term').astype(jnp.float32)]
    reduce_sum x0 -> x1, other arithmetic: none -> 23.3 us  [body(): jnp.sum(lax.all_gather(term_out.astype(jnp.bfloat16), 'term'), axis=0)]
where the time goes in v1:
time: 714 us
  waiting for transfers between devices  621 us (87%)
  local copies, waits for them, and re-layouts  29.6 us (4%)
  other arithmetic  27.8 us (4%)
  matrix products  21.7 us (3%)
  between operations  13.2 us (2%)
    all_gather x1, waiting for transfers between devices, body(): lax.all_gather(term_out.astype(jnp.bfloat16), 'term')  323 us
    all_gather x1, waiting for transfers between devices, body(): lax.all_gather(left_env[0], 'sec', axis=1, tiled=True)  159 us
    all_gather x1, waiting for transfers between devices, body(): lax.all_gather(right_env[0], 'sec', axis=1, tiled=True)  139 us
    reduce_sum x1, other arithmetic, body(): jnp.sum(lax.all_gather(term_out.astype(jnp.bfloat16), 'term'), axis=0)  23.3 us
    dot_general x1, matrix products, body(): jnp.einsum('kij,kjl->kil', chosen, half, preferred_element_type=jnp.float32)  21.7 us
  transfers between devices with their start and end apart: 3, of which 3 were waited for; matrix products, arithmetic and copies ran while one was open for 3% of the time, Pallas kernels for 0%

profile of v1, /device:TPU:1, one launch (start us, length us, event | category | flops | bytes accessed | tf_op | source)
XLA Modules:
  0.0 713.7 jit_solution(2164726085799862393)
XLA Ops:
  6.5 0.0 all-gather.9.cloned.1.call-start
  6.5 0.7 all-gather.9.cloned.1.call-update
  7.3 0.0 all-gather.7.cloned.1.call-start
  7.3 0.7 all-gather.7.cloned.1.call-update
  8.0 0.0 all-gather.11.cloned.1.call-start
  8.1 0.7 fusion.30
  8.7 0.0 copy-start
  8.7 0.0 copy-start.1
  8.7 10.6 %gather_fusion = bf16[24,512,512]{2,1,0:T(8,128)(2,1)} fusion(bf16[24,512,512]{2,1,0:T(8,128)(2,1)} %param.7, s32[1024]{0:T(1024)S(1)} %pad_clamp_fusion.1), kind=kCustom, calls=%fused_computation.2 | custom fusion | bytes 25165920 | tf_op jit(solution)/shard_map/jit(_take)/gather | solution.py:11
  19.4 0.0 copy-done
  19.4 0.0 copy-done.1
  19.4 138.6 %all-gather.9.cloned.1.call-done = bf16[1,16,512,512]{3,2,1,0:T(8,128)(2,1)} async-done(((bf16[1,16,16,512]{3,2,1,0:T(8,128)(2,1)}), bf16[1,16,512,512]{3,2,1,0:T(8,128)(2,1)}) %all-gather.9.cloned.1.call-update) | async-done | bytes 8388624 | tf_op jit(solution)/shard_map/all_gather | solution.py:14
  158.0 9.5 %gather_fusion.2 = bf16[24,512,512]{2,1,0:T(8,128)(2,1)} fusion(bf16[16,512,512]{2,1,0:T(8,128)(2,1)} %bitcast.16, s32[1024]{0:T(1024)S(1)} %get-tuple-element.12), kind=kCustom, calls=%fused_computation.1.clone | custom fusion | bytes 25165920 | tf_op jit(solution)/shard_map/jit(_take)/gather | solution.py:14
  167.4 158.8 %all-gather.7.cloned.1.call-done = bf16[1,16,512,512]{3,2,1,0:T(8,128)(2,1)} async-done(((bf16[1,16,16,512]{3,2,1,0:T(8,128)(2,1)}), bf16[1,16,512,512]{3,2,1,0:T(8,128)(2,1)}) %all-gather.7.cloned.1.call-update) | async-done | bytes 8388624 | tf_op jit(solution)/shard_map/all_gather | solution.py:18
  326.3 9.5 %gather_fusion.1 = bf16[24,512,512]{2,1,0:T(8,128)(2,1)} fusion(bf16[16,512,512]{2,1,0:T(8,128)(2,1)} %bitcast.17, s32[1024]{0:T(1024)S(1)} %get-tuple-element.13), kind=kCustom, calls=%fused_computation.clone | custom fusion | bytes 25165920 | tf_op jit(solution)/shard_map/jit(_take)/gather | solution.py:18
  335.8 21.7 %fusion.19 = bf16[24,512,512]{2,1,0:T(8,128)(2,1)} fusion(bf16[24,512,512]{2,1,0:T(8,128)(2,1)} %gather_fusion.2, bf16[24,512,512]{2,1,0:T(8,128)(2,1)} %gather_fusion, pred[24]{0:T(512)(128)(4,1)S(1)} %get-tuple-element.10, pred[24]{0:T(512)(128)(4,1)S(1)} %compare_and_fusion.2, bf16[24,512,512]{2,1,0:T(8,128)(2,1)} %gather_fusion.1, ...), kind=kOutput, calls=%fused_computation.12 | convolution fusion | flops 12916359168 | bytes 50331720 | tf_op jit(solution)/shard_map/kij,kjl->kil/dot_general | solution.py:19
  357.5 0.0 all-gather.11.cloned.1.call-update
  357.5 322.5 %all-gather.11.cloned.1.call-done = bf16[96,512,512]{2,1,0:T(8,128)(2,1)} async-done(((bf16[24,512,512]{2,1,0:T(8,128)(2,1)}), bf16[96,512,512]{2,1,0:T(8,128)(2,1)}) %all-gather.11.cloned.1.call-update) | async-done | bytes 50331664 | tf_op jit(solution)/shard_map/all_gather | solution.py:21
  680.0 23.3 %reduce_sum.12 = bf16[24,512,512]{2,1,0:T(8,128)(2,1)} reduce(bf16[4,24,512,512]{3,2,1,0:T(8,128)(2,1)} %bitcast.15, bf16[]{:T(256)} %constant.25.clone.1), dimensions={0}, to_apply=%region_0.0 | reduce | flops 18874368 | bytes 62914560 | tf_op jit(solution)/shard_map/reduce_sum | solution.py:21
  703.3 3.9 convert_convert_fusion
  (4 shorter events, 0.0 us)
Async XLA Ops:
  6.5 151.4 %all-gather.9.cloned.1.call-start = ((), (), s32[]{:S(2)}) async-start(), calls=%async_computation.1 | async-start | bytes 8650752 | tf_op jit(solution)/shard_map/all_gather | solution.py:14
  7.3 319.0 %all-gather.7.cloned.1.call-start = ((), (), s32[]{:S(2)}) async-start(), calls=%async_computation | async-start | bytes 8650752 | tf_op jit(solution)/shard_map/all_gather | solution.py:18
  8.0 672.0 %all-gather.11.cloned.1.call-start = ((), (), s32[]{:S(2)}) async-start(), calls=%async_computation.2 | async-start | bytes 62914560 | tf_op jit(solution)/shard_map/all_gather | solution.py:21
  8.7 10.6 %copy-start = (s32[24,2]{0,1:T(2,128)S(1)}, s32[24,2]{0,1:T(2,128)}, u32[]{:S(2)}) copy-start(s32[24,2]{0,1:T(2,128)} %param.8) | copy-start | bytes 580
  8.7 10.6 %copy-start.1 = (s32[1,24]{1,0:T(1,128)S(1)}, s32[1,24]{1,0:T(1,128)}, u32[]{:S(2)}) copy-start(s32[1,24]{1,0:T(1,128)} %param.9) | copy-start | bytes 292
Sparse Core Ops, SparseCore 0:
  9.0 148.9 all-gather.8
  159.6 166.6 all-gather.6
  357.6 322.3 all-gather.10
